TPU v7x, 128 devices: a whole 4x4x4 slice. The times are simulated.
128 devices in a mesh: chan: 16 (over y_lo, z, core), band: 8 (over x, y_hi).
Axes of the slice: x: 4, y: 4 (y_hi: 2, y_lo: 2; y = y_hi * 2 + y_lo), z: 4, core: 2. Of those that a mesh axis runs over, the one named last changes fastest.
Arguments:
- raw: bfloat16 [128, 2560, 2747], P(('chan', 'band')), may hold values from -600 to 600
- offsets: int32 [128], P(('chan', 'band')), may hold values from 0 to 127
- taps: bfloat16 [63], replicated, may hold values from -0.75 to 0.75
- partner: int32 [2, 16], replicated, may hold values from 0 to 15, as said below
Outputs:
- cross: float32 [2, 2, 128, 2560, 160], P(None, None, 'band', 'chan')
Inputs may be any that keep to these rules, and one draw needn't show every extreme that they name: For each round r there is one number M of 1 to 15 with partner[r, a] = a xor M for every block a; the two rounds' numbers differ.
All inputs are finite; a program needn't handle non-finite values.
Results may differ from a plain program's by a relative error of at most 0.0041.
Values may be sent and summed in bfloat16 or wider, within the bound.
No kernel may reach another device: no remote copies, remote signals or barrier semaphores. Data moves between devices by JAX's collectives and lax.ppermute only.
A program may use at most 128 MiB of HBM per device.

v0:
```python
import math
import jax
import jax.numpy as jnp
from jax import lax
from jax.sharding import PartitionSpec as P

DEC = 10
TAPS = 63
W = 256
NF = 128
HALF = 32


def mean_matrix(length, half):
    rows = jnp.arange(length, dtype=jnp.int32)[:, None]
    cols = jnp.arange(length, dtype=jnp.int32)[None, :]
    begins = jnp.clip(cols - half, 0, length - 2 * half - 1)
    inside = (rows >= begins) & (rows <= begins + 2 * half)
    return inside.astype(jnp.float32)


def dft_table(length, bins):
    samples = jnp.arange(length, dtype=jnp.int32)[:, None]
    freqs = jnp.arange(bins, dtype=jnp.int32)[None, :]
    phase = samples * freqs % length
    angle = phase.astype(jnp.float32) * (2.0 * math.pi / length)
    return jnp.concatenate([jnp.cos(angle), -jnp.sin(angle)], axis=1)


def filter_table(taps, phases):
    padded = jnp.pad(taps, (0, phases * DEC - TAPS))
    grid = padded.reshape(phases, DEC)
    rows = jnp.arange(W + phases - 1, dtype=jnp.int32)[:, None]
    cols = jnp.arange(W, dtype=jnp.int32)[None, :]
    onehot = (
        (rows - cols)[None, :, :] == jnp.arange(phases, dtype=jnp.int32)[:, None, None]
    ).astype(jnp.bfloat16)
    table = jnp.einsum("jqn,jr->qrn", onehot, grid, preferred_element_type=jnp.float32)
    return table.reshape((W + phases - 1) * DEC, W).astype(jnp.bfloat16)


def window_spectrum(segment, offset, table, level_matrix, transform):
    span = table.shape[0]
    piece = lax.dynamic_slice_in_dim(segment, offset, span, 1)
    decimated = jnp.dot(piece, table, preferred_element_type=jnp.float32)
    level = jnp.dot(jnp.abs(decimated), level_matrix, precision=lax.Precision.HIGHEST) / (
        2 * HALF + 1
    )
    normed = decimated / (level + 1e-05)
    spectrum = lax.dot_general(
        transform, normed, (((0,), (1,)), ((), ())), precision=lax.Precision.HIGHEST
    )
    return spectrum.reshape(2, NF, segment.shape[0]).astype(jnp.bfloat16)


def body(raw, offsets, taps, partner):
    phases = (TAPS + DEC - 1) // DEC
    table = filter_table(taps, phases)
    level_matrix = mean_matrix(W, HALF)
    transform = dft_table(W, NF)
    spectra = jnp.stack([window_spectrum(raw[0], offsets[0], table, level_matrix, transform)])
    chan_count = lax.axis_size("chan")
    band_count = lax.axis_size("band")
    window_count, part_count, bin_count, channel_count = spectra.shape
    arranged = spectra.reshape(
        window_count,
        part_count,
        band_count,
        bin_count // band_count,
        chan_count,
        channel_count // chan_count,
    )
    arranged = arranged.transpose(4, 2, 0, 1, 3, 5).reshape(
        chan_count * band_count * window_count,
        part_count,
        bin_count // band_count,
        channel_count // chan_count,
    )
    local = lax.all_to_all(arranged, ("chan", "band"), split_axis=0, concat_axis=0, tiled=True)
    width = local.shape[3]
    block = lax.axis_index("chan")
    block_count = partner.shape[1]
    own_partner = jnp.sum(
        jnp.where(jnp.arange(block_count, dtype=jnp.int32)[None, :] == block, partner, 0), axis=1
    )
    blank = jnp.zeros_like(local)
    carry = (blank, blank)
    piece = lax.all_gather(local, "chan", axis=3, tiled=True)
    span = piece.shape[3]
    chosen = []
    for round_index in range(2):
        placed = own_partner[round_index] * width
        inside = (placed >= 0) & (placed < span)
        window_rows = lax.dynamic_slice_in_dim(piece, jnp.clip(placed, 0, span - width), width, 3)
        chosen.append(jnp.where(inside, window_rows, carry[round_index]))
    first_other = chosen[0]
    second_other = chosen[1]
    factor = 1.0 / (W * math.sqrt(local.shape[0]))

    def stack_pair(other_rows):
        product = jnp.einsum(
            "wpfi,wqfj->fpqij", local, other_rows, preferred_element_type=jnp.float32
        )
        real_part = product[:, 0, 0] + product[:, 1, 1]
        imag_part = product[:, 1, 0] - product[:, 0, 1]
        return jnp.stack([real_part, imag_part]) * factor

    return jnp.stack([stack_pair(first_other), stack_pair(second_other)])


def solution(mesh):
    return jax.shard_map(
        body,
        mesh=mesh,
        in_specs=(P(("chan", "band"), None, None), P(("chan", "band")), P(), P()),
        out_specs=P(None, None, "band", "chan", None),
        check_vma=False,
    )
```

profile of v0, /device:TPU:1, one launch (start us, length us, event | category | flops | bytes accessed | tf_op | source)
XLA Modules:
  0.0 218.0 jit_solution(3624640159972781501)
XLA Ops:
  6.5 0.0 all-gather.2.cloned.1.call-start
  6.6 1.2 sine_negate_fusion
  8.5 0.7 pad.4
  9.1 0.1 reshape.230
  9.2 0.8 convert_bitcast_fusion
  10.0 0.5 convert_element_type.34
  10.5 7.2 %fusion = f32[2560,256]{1,0:T(8,128)S(1)} fusion(bf16[2620,256]{1,0:T(8,128)(2,1)S(1)} %convert_element_type.34, bf16[1,2560,2747]{1,2,0:T(8,128)(2,1)} %param.4, s32[]{:T(128)S(6)} %select_n.35), kind=kOutput, calls=%fused_computation | convolution fusion | flops 3434086400 | bytes 17397764 | tf_op jit(solution)/shard_map/dot_general | solution.py:45
  17.7 0.0 copy-start.1
  17.7 0.0 copy-start.2
  17.7 1.5 fusion.4
  19.2 0.0 copy-done.1
  19.2 0.0 copy-done.2
  19.2 4.4 %convolution_convert_fusion = bf16[256,2560]{1,0:T(8,128)(2,1)S(1)} fusion(f32[2560,256]{1,0:T(8,128)S(1)} %fusion.4, f32[256,128]{1,0:T(8,128)S(1)} %copy-done.1, f32[256,128]{1,0:T(8,128)S(1)} %copy-done.2), kind=kOutput, calls=%fused_computation.8 | convolution fusion | flops 2013986816 | bytes 4194304 | tf_op jit(solution)/shard_map/dot_general | solution.py:50
  23.6 2.6 %convert_element_type.36 = bf16[1,2,8,16,16,160]{5,4,3,2,1,0:T(8,128)(2,1)S(1)} reshape(bf16[256,2560]{1,0:T(8,128)(2,1)S(1)} %convolution_convert_fusion) | data formatting | bytes 2621440 | tf_op jit(solution)/shard_map/convert_element_type | solution.py:53
  26.2 0.7 copy.16
  26.9 2.4 %copy.17 = bf16[128,2,16,160]{3,1,2,0:T(2,128)(2,1)S(1)} copy(bf16[128,2,16,160]{3,2,1,0:T(8,128)(2,1)S(1)} %bitcast.54) | data formatting | bytes 2621440 | tf_op jit(solution)/shard_map/reshape | solution.py:73
  29.4 39.6 %all_to_all.5 = bf16[128,2,16,160]{3,1,2,0:T(2,128)(2,1)S(1)} all-to-all(bf16[128,2,16,160]{3,1,2,0:T(2,128)(2,1)S(1)} %copy.17), channel_id=1, replica_groups=mesh['chan'=16,'band'=8] {'chan','band'}, dimensions={0} | all-to-all | bytes 2621440 | tf_op jit(solution)/shard_map/all_to_all | solution.py:79
  68.9 3.8 %copy.18 = bf16[128,2,16,160]{0,3,1,2:T(8,128)(2,1)} copy(bf16[128,2,16,160]{3,1,2,0:T(2,128)(2,1)S(1)} %all_to_all.5) | data formatting | bytes 2621440 | tf_op jit(solution)/shard_map/all_to_all | solution.py:79
  72.8 0.0 all-gather.2.cloned.1.call-update
  72.8 0.1 select_reduce_fusion
  72.9 0.7 fusion.39
  74.9 107.6 %all-gather.2.cloned.1.call-done = bf16[128,2,16,2560]{0,3,1,2:T(8,128)(2,1)} async-done(((bf16[128,2,16,160]{0,3,1,2:T(8,128)(2,1)}), bf16[128,2,16,2560]{0,3,1,2:T(8,128)(2,1)}) %all-gather.2.cloned.1.call-update) | async-done | bytes 20971536 | tf_op jit(solution)/shard_map/all_gather | solution.py:88
  182.5 3.0 %convolution_bitcast_fusion.1 = f32[16,2,2,160,160]{3,4,1,2,0:T(8,128)S(1)} fusion(bf16[128,2,16,160,1]{3,1,2,0,4:T(2,128)(2,1)S(1)} %bitcast.52, bf16[128,2,16,2560]{0,3,1,2:T(8,128)(2,1)} %all-gather.2.cloned.1.call-done, s32[]{:T(128)} %bitcast.6, pred[]{:T(512)} %bitcast), kind=kOutput, calls=%fused_computation.11 | convolution fusion | flops 420085760 | bytes 9176064 | tf_op jit(solution)/shard_map/wpfi,wqfj->fpqij/dot_general | solution.py:101
  185.5 0.4 fusion.7
  185.9 0.4 fusion.9
  186.3 3.0 %convolution_bitcast_fusion = f32[16,2,2,160,160]{3,4,0,2,1:T(8,128)S(1)} fusion(bf16[128,2,16,160,1]{3,1,2,0,4:T(2,128)(2,1)S(1)} %bitcast.53, bf16[128,2,16,2560]{0,3,1,2:T(8,128)(2,1)} %all-gather.2.cloned.1.call-done, s32[]{:T(128)} %bitcast.14, pred[]{:T(512)} %bitcast.13), kind=kOutput, calls=%fused_computation.10 | convolution fusion | flops 420085760 | bytes 9176064 | tf_op jit(solution)/shard_map/wpfi,wqfj->fpqij/dot_general | solution.py:101
  189.4 2.3 %fusion.6 = (f32[1,1,16,160,160]{3,4,2,1,0:T(8,128)S(1)}, f32[1,1,16,160,160]{3,4,2,1,0:T(8,128)}) fusion(f32[16,2,2,160,160]{3,4,0,2,1:T(8,128)S(1)} %convolution_bitcast_fusion), kind=kLoop, calls=%fused_computation.15 | loop fusion | flops 819200 | bytes 9830400 | tf_op jit(solution)/shard_map/stack | solution.py:106
  191.7 0.8 maximum_multiply_fusion
  192.5 0.9 copy-done
  193.4 0.8 maximum_multiply_fusion.1
  194.3 4.8 %pad_maximum_fusion = f32[2,2,16,160,160]{3,4,2,1,0:T(8,128)} fusion(f32[1,2,16,160,160]{3,4,2,1,0:T(8,128)S(1)} %maximum_multiply_fusion.1, f32[1,2,16,160,160]{3,4,2,1,0:T(8,128)S(1)} %maximum_multiply_fusion), kind=kLoop, calls=%fused_computation.3 | loop fusion | flops 1638400 | bytes 13107200 | tf_op jit(solution)/shard_map/stack | solution.py:108
  199.1 12.1 %copy.24 = f32[2,2,16,160,160]{4,3,2,1,0:T(8,128)} copy(f32[2,2,16,160,160]{3,4,2,1,0:T(8,128)} %pad_maximum_fusion) | data formatting | bytes 13107200 | tf_op jit(solution)/shard_map/stack | solution.py:108
  (6 shorter events, 0.0 us)
Async XLA Ops:
  6.5 176.0 %all-gather.2.cloned.1.call-start = ((), (), s32[]{:S(2)}) async-start(), calls=%async_computation.1 | async-start | bytes 22282240 | tf_op jit(solution)/shard_map/all_gather | solution.py:88
  17.7 1.5 copy-start.1
  17.7 1.5 copy-start.2
  68.9 3.9 %copy-start.3 = (s32[2,16]{1,0:T(2,128)S(1)}, s32[2,16]{1,0:T(2,128)}, u32[]{:S(2)}) copy-start(s32[2,16]{1,0:T(2,128)} %param.7) | copy-start | bytes 388
  191.7 1.7 copy-start
Sparse Core Ops, SparseCore 0:
  72.9 109.5 all-gather.1
where the time goes:
time: 218 us
  waiting for transfers between devices  108 us (50%)
  blocking collectives  39.6 us (18%)
  local copies, waits for them, and re-layouts  24.4 us (11%)
  matrix products  19.9 us (9%)
  between operations  15.5 us (7%)
  other arithmetic  11 us (5%)
    all_gather x1, waiting for transfers between devices, body(): piece = lax.all_gather(local, 'chan', axis=3, tiled=True)  108 us
    all_to_all x1, blocking collectives, body(): lax.all_to_all(arranged, ('chan', 'band'), split_axis=0, concat_axis=0, t...  39.6 us
    another operation x1, local copies, waits for them, and re-layouts, body(): return jnp.stack([stack_pair(first_other), stack_pair(second_other)])  12.1 us
    dot_general x1, matrix products, window_spectrum(): decimated = jnp.dot(piece, table, preferred_element_type=jnp.float32)  7.16 us
    dot_general x2, matrix products, stack_pair(): jnp.einsum('wpfi,wqfj->fpqij', local, other_rows, preferred_element_type=...  6.08 us
    another operation x1, other arithmetic, body(): return jnp.stack([stack_pair(first_other), stack_pair(second_other)])  4.8 us
    dot_general x1, matrix products, window_spectrum(): lax.dot_general(transform, normed, (((0,), (1,)), ((), ())), precision=la...  4.41 us
  transfers between devices with their start and end apart: 1, of which 1 were waited for; matrix products, arithmetic and copies ran while one was open for 0% of the time, Pallas kernels for 0%

commit v1 on v0

--- a/solution.py
+++ b/solution.py
@@ -1,3 +1,4 @@
+import functools
 import math
 import jax
 import jax.numpy as jnp
@@ -9,6 +10,16 @@
 W = 256
 NF = 128
 HALF = 32
+
+
+def rates_find(piece_in, dim_k):
+    base_arr = jnp.stack(tuple((piece_in for _ in range(jax.lax.axis_size("chan")))))
+    block_last = jax.lax.all_to_all(base_arr, "chan", 0, 0)
+    high = jnp.concatenate(block_last, axis=dim_k)
+    return high
+
+
+series_all_choose = functools.partial(rates_find, dim_k=3)
 
 
 def mean_matrix(length, half):
@@ -85,7 +96,7 @@
     )
     blank = jnp.zeros_like(local)
     carry = (blank, blank)
-    piece = lax.all_gather(local, "chan", axis=3, tiled=True)
+    piece = series_all_choose(local)
     span = piece.shape[3]
     chosen = []
     for round_index in range(2):

time: 218 us -> 454 us (2.08)
  waiting for transfers between devices: 108 us -> 323 us
  local copies, waits for them, and re-layouts: 24.4 us -> 48.7 us
  between operations: 15.5 us -> 2.14 us
  starting transfers between devices: 0.01 us -> 7.35 us
    all_to_all x0 -> x1, waiting for transfers between devices: none -> 323 us  [rates_find(): block_last = jax.lax.all_to_all(base_arr, 'chan', 0, 0)]
    all_gather x1 -> x0, waiting for transfers between devices: 108 us -> none  [body(): piece = lax.all_gather(local, 'chan', axis=3, tiled=True)]
    reshape x0 -> x1, local copies, waits for them, and re-layouts: none -> 11.7 us  [rates_find(): high = jnp.concatenate(block_last, axis=dim_k)]
    another operation x0 -> x1, local copies, waits for them, and re-layouts: none -> 8.08 us  [rates_find(): jnp.stack(tuple((piece_in for _ in range(jax.lax.axis_size('chan')))))]
    all_to_all x0 -> x1, starting transfers between devices: none -> 7.35 us  [rates_find(): block_last = jax.lax.all_to_all(base_arr, 'chan', 0, 0)]
    unnamed x8 -> x14, local copies, waits for them, and re-layouts: 0.91 us -> 7.09 us
where the time goes in v1:
time: 454 us; the launch traced here: 452 us
  waiting for transfers between devices  323 us (71%)
  local copies, waits for them, and re-layouts  48.7 us (11%)
  blocking collectives  39.6 us (9%)
  matrix products  18.6 us (4%)
  other arithmetic  12.9 us (3%)
  starting transfers between devices  7.35 us (2%)
    all_to_all x1, waiting for transfers between devices, rates_find(): block_last = jax.lax.all_to_all(base_arr, 'chan', 0, 0)  323 us
    all_to_all x1, blocking collectives, body(): lax.all_to_all(arranged, ('chan', 'band'), split_axis=0, concat_axis=0, t...  39.6 us
    another operation x1, local copies, waits for them, and re-layouts, body(): return jnp.stack([stack_pair(first_other), stack_pair(second_other)])  12.1 us
    reshape x1, local copies, waits for them, and re-layouts, rates_find(): high = jnp.concatenate(block_last, axis=dim_k)  11.7 us
  transfers between devices with their start and end apart: 1, of which 1 were waited for; matrix products, arithmetic and copies ran while one was open for 0% of the time, Pallas kernels for 0%

profile of v1, /device:TPU:1, one launch (start us, length us, event | category | flops | bytes accessed | tf_op | source)
XLA Modules:
  0.0 452.3 jit_solution(15034331084163549206)
XLA Ops:
  0.0 1.2 sine_negate_fusion
  1.9 0.7 pad.4
  2.6 0.1 reshape.240
  2.7 0.8 convert_bitcast_fusion
  3.5 0.5 convert_element_type.34
  4.0 7.2 %fusion = f32[2560,256]{1,0:T(8,128)S(1)} fusion(bf16[2620,256]{1,0:T(8,128)(2,1)S(1)} %convert_element_type.34, bf16[1,2560,2747]{1,2,0:T(8,128)(2,1)} %param.4, s32[]{:T(128)S(6)} %select_n.35), kind=kOutput, calls=%fused_computation | convolution fusion | flops 3434086400 | bytes 17397764 | tf_op jit(solution)/shard_map/dot_general | solution.py:56
  11.1 0.0 copy-start.4
  11.2 1.5 fusion.4
  12.7 4.4 convolution_convert_fusion
  17.1 2.6 convert_element_type.36
  19.7 0.7 copy.16
  20.4 2.4 copy.17
  22.8 39.6 %all_to_all.10 = bf16[128,2,16,160]{3,1,2,0:T(2,128)(2,1)S(1)} all-to-all(bf16[128,2,16,160]{3,1,2,0:T(2,128)(2,1)S(1)} %copy.17), channel_id=1, replica_groups=mesh['chan'=16,'band'=8] {'chan','band'}, dimensions={0} | all-to-all | bytes 2621440 | tf_op jit(solution)/shard_map/all_to_all | solution.py:90
  62.4 2.1 copy.18
  64.5 8.1 %stack.16 = bf16[16,128,2,16,160]{1,4,2,3,0:T(8,128)(2,1)} broadcast(bf16[128,2,16,160]{0,3,1,2:T(8,128)(2,1)S(1)} %copy.18), dimensions={1,2,3,4} | broadcast | bytes 22282240 | tf_op jit(solution)/shard_map/stack | solution.py:16
  72.6 7.3 %all-to-all-start.1 = ((bf16[16,128,2,16,160]{1,4,2,3,0:T(8,128)(2,1)}), bf16[16,128,2,16,160]{1,4,2,3,0:T(8,128)(2,1)}, u32[]{:S(2)}, u32[]{:S(2)}) async-start(bf16[16,128,2,16,160]{1,4,2,3,0:T(8,128)(2,1)} %stack.16), calls=%async_computation.1 | async-start | bytes 41943040 | tf_op jit(solution)/shard_map/all_to_all | solution.py:17
  80.0 0.1 select_reduce_fusion
  80.1 0.6 fusion.39
  82.0 323.0 %all-to-all-done.1 = bf16[16,128,2,16,160]{1,4,2,3,0:T(8,128)(2,1)} async-done(((bf16[16,128,2,16,160]{1,4,2,3,0:T(8,128)(2,1)}), bf16[16,128,2,16,160]{1,4,2,3,0:T(8,128)(2,1)}, u32[]{:S(2)}, u32[]{:S(2)}) %all-to-all-start.1) | async-done | bytes 20971552 | tf_op jit(solution)/shard_map/all_to_all | solution.py:17
  405.0 11.7 %copy.19 = bf16[128,2,16,16,160]{0,4,3,1,2:T(8,128)(2,1)S(1)} copy(bf16[128,2,16,16,160]{0,4,1,2,3:T(8,128)(2,1)} %bitcast.6) | data formatting | bytes 41943040 | tf_op jit(solution)/shard_map/reshape | solution.py:18
  416.7 1.8 convolution_bitcast_fusion.1
  418.5 5.2 %copy-done = bf16[128,2,16,16,160]{0,4,3,1,2:T(8,128)(2,1)} copy-done((bf16[128,2,16,16,160]{0,4,3,1,2:T(8,128)(2,1)}, bf16[128,2,16,16,160]{0,4,3,1,2:T(8,128)(2,1)S(1)}, u32[]{:S(2)}) %copy-start) | copy-done | bytes 20971544
  423.7 0.4 fusion.7
  424.1 1.9 fusion.9
  426.0 3.0 convolution_bitcast_fusion
  429.0 3.3 fusion.6
  432.3 0.6 maximum_multiply_fusion
  433.0 1.1 copy-done.2
  434.1 0.8 copy-done.3
  434.9 0.5 maximum_multiply_fusion.1
  435.4 4.8 %pad_maximum_fusion = f32[2,2,16,160,160]{3,4,2,1,0:T(8,128)} fusion(f32[1,2,16,160,160]{3,4,2,1,0:T(8,128)S(1)} %maximum_multiply_fusion.1, f32[1,2,16,160,160]{3,4,2,1,0:T(8,128)S(1)} %maximum_multiply_fusion), kind=kLoop, calls=%fused_computation.3 | loop fusion | flops 1638400 | bytes 13107200 | tf_op jit(solution)/shard_map/stack | solution.py:119
  440.2 12.1 %copy.25 = f32[2,2,16,160,160]{4,3,2,1,0:T(8,128)} copy(f32[2,2,16,160,160]{3,4,2,1,0:T(8,128)} %pad_maximum_fusion) | data formatting | bytes 13107200 | tf_op jit(solution)/shard_map/stack | solution.py:119
  (13 shorter events, 0.1 us)
Async XLA Ops:
  11.1 1.5 copy-start.4
  11.1 1.5 copy-start.5
  72.6 7.4 %copy-start.6 = (s32[2,16]{1,0:T(2,128)S(1)}, s32[2,16]{1,0:T(2,128)}, u32[]{:S(2)}) copy-start(s32[2,16]{1,0:T(2,128)} %param.7) | copy-start | bytes 388
  72.6 332.4 %all-to-all-start.1 = ((bf16[16,128,2,16,160]{1,4,2,3,0:T(8,128)(2,1)}), bf16[16,128,2,16,160]{1,4,2,3,0:T(8,128)(2,1)}, u32[]{:S(2)}, u32[]{:S(2)}) async-start(bf16[16,128,2,16,160]{1,4,2,3,0:T(8,128)(2,1)} %stack.16), calls=%async_computation.1 | async-start | bytes 41943040 | tf_op jit(solution)/shard_map/all_to_all | solution.py:17
  416.7 7.0 %copy-start = (bf16[128,2,16,16,160]{0,4,3,1,2:T(8,128)(2,1)}, bf16[128,2,16,16,160]{0,4,3,1,2:T(8,128)(2,1)S(1)}, u32[]{:S(2)}) copy-start(bf16[128,2,16,16,160]{0,4,3,1,2:T(8,128)(2,1)S(1)} %copy.19) | copy-start | bytes 62914564
  429.0 3.3 copy-start.1
  432.3 1.7 copy-start.2
  432.3 2.5 copy-start.3
